TPU v7x, 32 devices: a whole 2x2x4 slice. The times are simulated.
32 devices in a mesh: seq: 16 (over z, y, core), mp: 2 (over x).
Axes of the slice: x: 2, y: 2, z: 4, core: 2. Of those that a mesh axis runs over, the one named last changes fastest.
Arguments:
- tokens: bfloat16 [4096, 2048], P('seq'), may hold values from -25 to 25
- lengths: int32 [32], replicated, may hold values from 1 to 1024, 4096 in all
- prefix_cache: bfloat16 [4, 2048, 512], P(None, 'seq'), may hold values from -1000 to 1000
- attn_gain: bfloat16 [2048], replicated, may hold values from 0.25 to 1.75
- w_query: bfloat16 [2048, 2048], P(None, 'mp'), may hold values from -0.25 to 0.25
- w_keyval: bfloat16 [2048, 512], replicated, may hold values from -0.125 to 0.125
- w_out: bfloat16 [2048, 2048], P('mp'), may hold values from -0.25 to 0.25
- final_gain: bfloat16 [2048], replicated, may hold values from 0.25 to 1.75
- w_head: bfloat16 [2048, 32000], P(None, ('seq', 'mp')), may hold values from -0.4375 to 0.4375
Outputs:
- hidden: bfloat16 [4096, 2048], P('seq', 'mp')
- suffix_cache: bfloat16 [4096, 512], P('seq')
- last_normed: bfloat16 [32, 2048], replicated
- greatest: float32 [32], replicated
Inputs may be any that keep to these rules, and one draw needn't show every extreme that they name: The lengths sum to 4096 and one of them equals 1024.
All inputs are finite; a program needn't handle non-finite values.
Results may differ from a plain program's by a relative error of at most 0.013.
Values may be sent and summed in bfloat16 or wider, within the bound.
No kernel may reach another device: no remote copies, remote signals or barrier semaphores. Data moves between devices by JAX's collectives and lax.ppermute only.
A program may use at most 64 MiB of HBM per device.

v0:
```python
import math
import jax
import jax.numpy as jnp
from jax import lax
from jax.sharding import PartitionSpec as P

QH = 32
KVH = 4
HD = 64
G = 4
RPG = 8
P_SIZE = 2048
MOST = 1024
PREFIX_CHUNK = 512
epsilon = 1e-05


def rotate(source, places, head_count):
    half_dim = HD // 2
    row_count = source.shape[0]
    reshaped = source.reshape(row_count, head_count, HD)
    frequency = 10000.0 ** (-(jnp.arange(half_dim, dtype=jnp.float32) * 2.0 / HD))
    angles = places.astype(jnp.float32)[:, None] * frequency[None, :]
    cos_table = jnp.cos(angles)[:, None, :]
    sine_table = jnp.sin(angles)[:, None, :]
    leading = reshaped[..., :half_dim]
    second = reshaped[..., half_dim:]
    joined = jnp.concatenate(
        [leading * cos_table - second * sine_table, second * cos_table + leading * sine_table], -1
    )
    return joined.reshape(row_count, head_count * HD)


def attend(running, queries, kv_block, allowed):
    old_max, old_sum, numerator = running
    half_width = kv_block.shape[1] // 2
    kv_heads = queries.shape[1]
    key_rows = kv_block[:, :half_width].reshape(kv_block.shape[0], kv_heads, HD)
    val_rows = kv_block[:, half_width:].reshape(kv_block.shape[0], kv_heads, HD)
    scores = jnp.einsum("qgrd,ngd->grqn", queries, key_rows, preferred_element_type=jnp.float32) * (
        1.0 / math.sqrt(HD)
    )
    scores = jnp.where(allowed[None, None], scores, -jnp.inf)
    new_max = jnp.maximum(old_max, jnp.max(scores, -1))
    factor = jnp.exp(old_max - new_max)
    weights = jnp.exp(scores - new_max[..., None])
    new_sum = old_sum * factor + jnp.sum(weights, -1)
    numerator = numerator * factor[..., None] + jnp.einsum(
        "grqn,ngd->grqd", weights.astype(jnp.bfloat16), val_rows, preferred_element_type=jnp.float32
    )
    return (new_max, new_sum, numerator)


def shifted_back(block, axis, distance):
    count = lax.axis_size(axis)
    route = [(i, i + distance) for i in range(count - distance)]
    return lax.ppermute(block, axis, route)


def per_device(
    tokens, lengths, prefix_cache, attn_gain, w_query, w_keyval, w_out, final_gain, w_head
):
    token_rows = tokens.shape[0]
    model_width = tokens.shape[1]
    seq_devices = lax.axis_size("seq")
    seq_index = lax.axis_index("seq")
    mp_index = lax.axis_index("mp")
    part_width = model_width // lax.axis_size("mp")
    query_heads = w_query.shape[1] // HD
    group_size = QH // KVH
    kv_heads = max(1, query_heads // group_size)
    repeat_count = query_heads // kv_heads
    kv_first = mp_index * query_heads // group_size
    kv_width = KVH * HD
    request_count = lengths.shape[0]
    back_blocks = min(seq_devices - 1, -(-(MOST - 1) // token_rows))
    own_prefix = jnp.concatenate(
        [
            lax.dynamic_slice_in_dim(prefix_cache, kv_first * HD, kv_heads * HD, 2),
            lax.dynamic_slice_in_dim(prefix_cache, kv_width + kv_first * HD, kv_heads * HD, 2),
        ],
        2,
    )
    prefix_rows = own_prefix.shape[1]
    block_width = own_prefix.shape[2]
    all_prefix = lax.all_gather(own_prefix, "seq", axis=0)
    activations = tokens.astype(jnp.float32)
    normed = (
        activations
        * lax.rsqrt(jnp.mean(activations * activations, -1, keepdims=True) + epsilon)
        * attn_gain.astype(jnp.float32)
    ).astype(jnp.bfloat16)
    request_end = jnp.cumsum(lengths)
    starts = request_end - lengths
    position = seq_index * token_rows + jnp.arange(token_rows, dtype=jnp.int32)
    request = jnp.sum((position[:, None] >= request_end[None, :]).astype(jnp.int32), 1)
    request_table = request[:, None] == jnp.arange(request_count, dtype=jnp.int32)[None, :]
    offset = position - jnp.sum(jnp.where(request_table, starts[None, :], 0), 1)
    group_of = request // RPG
    keyval = jnp.dot(normed, w_keyval, preferred_element_type=jnp.float32)
    key_rows = rotate(keyval[:, :kv_width], P_SIZE + offset, KVH).astype(jnp.bfloat16)
    val_rows = keyval[:, kv_width:].astype(jnp.bfloat16)
    suffix_cache = jnp.concatenate([key_rows, val_rows], 1)
    own_suffix = jnp.concatenate(
        [
            lax.dynamic_slice_in_dim(key_rows, kv_first * HD, kv_heads * HD, 1),
            lax.dynamic_slice_in_dim(val_rows, kv_first * HD, kv_heads * HD, 1),
        ],
        1,
    )
    earlier = [own_suffix] + [
        shifted_back(own_suffix, "seq", distance) for distance in range(1, back_blocks + 1)
    ]
    suffix_window = jnp.stack(earlier, 0)
    query_full = jnp.dot(normed, w_query, preferred_element_type=jnp.float32)
    queries = (
        rotate(query_full, P_SIZE + offset, query_heads)
        .astype(jnp.bfloat16)
        .reshape(token_rows, kv_heads, repeat_count, HD)
    )
    running = (
        jnp.full((kv_heads, repeat_count, token_rows), -1e30, jnp.float32),
        jnp.zeros((kv_heads, repeat_count, token_rows), jnp.float32),
        jnp.zeros((kv_heads, repeat_count, token_rows, HD), jnp.float32),
    )
    sources_per_chunk = max(1, PREFIX_CHUNK // prefix_rows)
    chunks_per_group = seq_devices // sources_per_chunk
    first_group = group_of[0]
    last_group = group_of[token_rows - 1]

    def prefix_step(chunk, state_now):
        group = chunk // chunks_per_group
        part = chunk % chunks_per_group
        block = lax.dynamic_slice(
            all_prefix,
            (part * sources_per_chunk, group, 0, 0),
            (sources_per_chunk, 1, prefix_rows, block_width),
        ).reshape(sources_per_chunk * prefix_rows, block_width)
        allowed = jnp.broadcast_to(
            (group_of == group)[:, None], (token_rows, sources_per_chunk * prefix_rows)
        )
        return attend(state_now, queries, block, allowed)

    running = lax.fori_loop(
        first_group * chunks_per_group, (last_group + 1) * chunks_per_group, prefix_step, running
    )
    first_block = starts[request[0]] // token_rows
    back_needed = jnp.minimum(seq_index - first_block, back_blocks)

    def suffix_step(distance, state_now):
        source_dev = seq_index - distance
        key_place = source_dev * token_rows + jnp.arange(token_rows, dtype=jnp.int32)
        key_request = jnp.sum((key_place[:, None] >= request_end[None, :]).astype(jnp.int32), 1)
        allowed = (
            (request[:, None] == key_request[None, :])
            & (key_place[None, :] <= position[:, None])
            & (source_dev >= 0)
        )
        block = lax.dynamic_index_in_dim(suffix_window, distance, 0, keepdims=False)
        return attend(state_now, queries, block, allowed)

    running = lax.fori_loop(0, back_needed + 1, suffix_step, running)
    final_max, final_sum, numerator = running
    context = numerator / final_sum[..., None]
    context = (
        jnp.transpose(context, (2, 0, 1, 3))
        .reshape(token_rows, query_heads * HD)
        .astype(jnp.bfloat16)
    )
    mixture = jnp.dot(context, w_out, preferred_element_type=jnp.float32)
    mixture = lax.psum_scatter(
        mixture.astype(jnp.bfloat16), "mp", scatter_dimension=1, tiled=True
    ).astype(jnp.float32)
    own_columns = lax.dynamic_slice_in_dim(activations, mp_index * part_width, part_width, 1)
    hidden = (own_columns + mixture).astype(jnp.bfloat16)
    local_last = request_end - 1 - seq_index * token_rows
    onehot = (local_last[:, None] == jnp.arange(token_rows, dtype=jnp.int32)[None, :]).astype(
        jnp.bfloat16
    )
    last_part = jnp.dot(onehot, hidden, preferred_element_type=jnp.float32).astype(jnp.bfloat16)
    last_part = lax.psum(last_part, "seq")
    last_rows = lax.all_gather(last_part, "mp", axis=1, tiled=True).astype(jnp.float32)
    inv_rms = lax.rsqrt(jnp.mean(last_rows * last_rows, -1, keepdims=True) + epsilon)
    last_normed = (last_rows * final_gain.astype(jnp.float32) * inv_rms).astype(jnp.bfloat16)
    logits = jnp.dot(last_normed, w_head, preferred_element_type=jnp.float32)
    greatest = lax.pmax(jnp.max(logits, -1), ("seq", "mp"))
    return (hidden, suffix_cache, last_normed, greatest)


def solution(mesh):
    return jax.shard_map(
        per_device,
        mesh=mesh,
        in_specs=(
            P("seq", None),
            P(),
            P(None, "seq", None),
            P(),
            P(None, "mp"),
            P(),
            P("mp", None),
            P(),
            P(None, ("seq", "mp")),
        ),
        out_specs=(P("seq", "mp"), P("seq", None), P(), P()),
        check_vma=False,
    )
```

profile of v0, /device:TPU:0, one launch (start us, length us, event | category | flops | bytes accessed | tf_op | source)
XLA Modules:
  0.0 349.4 jit_solution(14837220267693971893)
XLA Ops:
  7.3 1.3 constant_dynamic-slice_fusion.5
  8.6 0.7 pad_maximum_fusion.1
  9.4 0.7 convert_element_type.75
  10.1 1.5 multiply_reduce_fusion
  11.6 2.0 fusion.24
  13.7 0.7 slice.63
  14.7 1.1 copy.41
  15.9 1.2 add_subtract_fusion
  17.3 0.5 copy-done.14
  18.0 0.5 copy-done.8
  18.8 0.7 pad_maximum_fusion.4
  19.5 3.0 collective-permute-start
  22.5 4.4 %collective-permute-start.1 = (bf16[256,256]{1,0:T(8,128)(2,1)}, bf16[256,256]{1,0:T(8,128)(2,1)}, u32[]{:S(2)}, u32[]{:S(2)}) collective-permute-start(bf16[256,256]{1,0:T(8,128)(2,1)} %pad_maximum_fusion.4), channel_id=1, source_target_pairs={{0,4},{2,6},{4,8},{6,10},{8,12},{10,14},{12,16},{14,18},{16,20},{1... | collective-permute-start | bytes 393224 | tf_op jit(solution)/shard_map/ppermute | solution.py:57
  26.9 4.4 %collective-permute-start.2 = (bf16[256,256]{1,0:T(8,128)(2,1)}, bf16[256,256]{1,0:T(8,128)(2,1)}, u32[]{:S(2)}, u32[]{:S(2)}) collective-permute-start(bf16[256,256]{1,0:T(8,128)(2,1)} %pad_maximum_fusion.4), channel_id=1, source_target_pairs={{0,6},{2,8},{4,10},{6,12},{8,14},{10,16},{12,18},{14,20},{16,22},{... | collective-permute-start | bytes 393224 | tf_op jit(solution)/shard_map/ppermute | solution.py:57
  31.4 3.5 collective-permute-start.3
  34.8 0.7 bitcast_dynamic-update-slice_fusion.4
  35.5 4.0 %fusion.25 = f32[256,1024]{0,1:T(8,128)S(1)} fusion(bf16[2048,1024]{1,0:T(8,128)(2,1)} %param.17, f32[2048]{0:T(1024)S(1)} %convert_element_type.75, f32[256]{0:T(256)} %copy-done.17, bf16[256,2048]{1,0:T(8,128)(2,1)S(1)} %copy-done.4), kind=kOutput, calls=%fused_computation.46 | convolution fusion | flops 1075838976 | bytes 6300672 | tf_op jit(solution)/shard_map/dot_general | solution.py:115
  39.7 0.6 fusion.32
  40.3 0.6 slice.50
  42.8 0.6 dynamic_slice.31
  47.2 1.6 bitcast_dynamic-update-slice_fusion.3
  48.8 1.6 bitcast_dynamic-update-slice_fusion.2
  50.3 1.6 bitcast_dynamic-update-slice_fusion.1
  51.9 1.6 bitcast_dynamic-update-slice_fusion
  53.5 13.9 %all-gather.3.cloned.1.call-done = bf16[64,128,256]{2,1,0:T(8,128)(2,1)} async-done(((bf16[4,128,256]{2,1,0:T(8,128)(2,1)}), bf16[64,128,256]{2,1,0:T(8,128)(2,1)}) %all-gather.3.cloned.1.call-update) | async-done | bytes 4194320 | tf_op jit(solution)/shard_map/all_gather | solution.py:86
  67.4 1.1 broadcast_in_dim.52
  68.6 49.2 %while.31 = (s32[]{:T(128)}, f32[2,8,256]{2,1,0:T(8,128)S(1)}, f32[2,8,256]{2,1,0:T(8,128)S(1)}, f32[2,8,256,64]{2,3,1,0:T(8,128)}, s32[]{:T(128)}, /*index=5*/s...) while((s32[]{:T(128)}, f32[2,8,256]{2,1,0:T(8,128)S(1)}, ...), condition=%wide.region_7.8_spmd, body=%wide.region_4.7_spmd.sunk | while | flops 560472320 | bytes 63441352 | solution.py:144
  68.6 1.0 constant_dynamic-slice_fusion.8
  69.7 1.3 bitcast_reduce_fusion.2
  71.0 1.7 fusion.66
  72.7 1.5 copy-done.1
  74.4 6.5 %fusion.67 = f32[2,8,256,64]{2,3,1,0:T(8,128)} fusion(bf16[512,2,64,1]{0,2,3,1:T(8,128)(2,1)S(1)} %bitcast.123, f32[2,512,256,8]{2,1,3,0:T(8,128)} %copy-done.1, f32[2,8,256]{2,1,0:T(8,128)S(1)} %max.14, pred[256]{0:T(512)(128)(4,1)S(1)} %broadcast_compare_fusion.2, f32[2,8,256,64]{2,3,1,0:T(8,128)} %get-tuple-element.501, ...), kind=kOutput, calls=%fused_computation.9.clone.1 | convolution fusion | flops 277348352 | bytes 10649856 | tf_op jit(solution)/shard_map/while/body/grqn,ngd->grqd/dot_general | solution.py:48
  80.9 1.0 constant_dynamic-slice_fusion.8
  82.0 1.3 bitcast_reduce_fusion.2
  83.3 1.7 fusion.66
  85.0 1.5 copy-done.1
  86.7 6.5 %fusion.67 = f32[2,8,256,64]{2,3,1,0:T(8,128)} fusion(bf16[512,2,64,1]{0,2,3,1:T(8,128)(2,1)S(1)} %bitcast.123, f32[2,512,256,8]{2,1,3,0:T(8,128)} %copy-done.1, f32[2,8,256]{2,1,0:T(8,128)S(1)} %max.14, pred[256]{0:T(512)(128)(4,1)S(1)} %broadcast_compare_fusion.2, f32[2,8,256,64]{2,3,1,0:T(8,128)} %get-tuple-element.501, ...), kind=kOutput, calls=%fused_computation.9.clone.1 | convolution fusion | flops 277348352 | bytes 10649856 | tf_op jit(solution)/shard_map/while/body/grqn,ngd->grqd/dot_general | solution.py:48
  93.2 1.0 constant_dynamic-slice_fusion.8
  94.3 1.3 bitcast_reduce_fusion.2
  95.6 1.7 fusion.66
  97.3 1.5 copy-done.1
  99.0 6.5 %fusion.67 = f32[2,8,256,64]{2,3,1,0:T(8,128)} fusion(bf16[512,2,64,1]{0,2,3,1:T(8,128)(2,1)S(1)} %bitcast.123, f32[2,512,256,8]{2,1,3,0:T(8,128)} %copy-done.1, f32[2,8,256]{2,1,0:T(8,128)S(1)} %max.14, pred[256]{0:T(512)(128)(4,1)S(1)} %broadcast_compare_fusion.2, f32[2,8,256,64]{2,3,1,0:T(8,128)} %get-tuple-element.501, ...), kind=kOutput, calls=%fused_computation.9.clone.1 | convolution fusion | flops 277348352 | bytes 10649856 | tf_op jit(solution)/shard_map/while/body/grqn,ngd->grqd/dot_general | solution.py:48
  105.5 1.0 constant_dynamic-slice_fusion.8
  106.6 1.3 bitcast_reduce_fusion.2
  108.0 1.7 fusion.66
  109.6 1.5 copy-done.1
  111.3 6.5 %fusion.67 = f32[2,8,256,64]{2,3,1,0:T(8,128)} fusion(bf16[512,2,64,1]{0,2,3,1:T(8,128)(2,1)S(1)} %bitcast.123, f32[2,512,256,8]{2,1,3,0:T(8,128)} %copy-done.1, f32[2,8,256]{2,1,0:T(8,128)S(1)} %max.14, pred[256]{0:T(512)(128)(4,1)S(1)} %broadcast_compare_fusion.2, f32[2,8,256,64]{2,3,1,0:T(8,128)} %get-tuple-element.501, ...), kind=kOutput, calls=%fused_computation.9.clone.1 | convolution fusion | flops 277348352 | bytes 10649856 | tf_op jit(solution)/shard_map/while/body/grqn,ngd->grqd/dot_general | solution.py:48
  117.8 5.3 %while.32 = (s32[]{:T(128)}, f32[2,8,256]{2,1,0:T(8,128)S(1)}, f32[2,8,256]{2,1,0:T(8,128)S(1)}, f32[2,8,256,64]{2,3,1,0:T(8,128)}, s32[]{:T(128)}, /*index=5*/s...) while((s32[]{:T(128)}, f32[2,8,256]{2,1,0:T(8,128)S(1)}, ...), condition=%wide.region_12.13_spmd.clone, body=%wide.region_8.12_spmd.clone.sunk | while | flops 280789248 | bytes 25043356 | solution.py:162
  118.1 0.9 constant_dynamic-slice_fusion.9
  119.1 0.8 fusion.73
  119.9 0.9 fusion.74
  120.8 1.2 fusion.75
  122.0 1.0 copy-done.3
  123.1 1.3 divide_convert_fusion
  124.4 4.6 %convolution_convert_fusion = bf16[256,2048]{1,0:T(8,128)(2,1)} fusion(bf16[256,1024]{0,1:T(8,128)(2,1)S(1)} %bitcast.126, bf16[1024,2048]{1,0:T(8,128)(2,1)} %param.19), kind=kOutput, calls=%fused_computation.33 | convolution fusion | flops 1074266112 | bytes 5767168 | tf_op jit(solution)/shard_map/dot_general | solution.py:170
  129.1 1.6 convert_element_type.73
  130.6 71.8 %reduce-scatter.2.cloned.1.call-done = bf16[256,1024]{1,0:T(8,128)(2,1)} async-done(((bf16[256,2048]{1,0:T(8,128)(2,1)}), bf16[256,1024]{1,0:T(8,128)(2,1)}) %reduce-scatter.2.cloned.1.call-update) | async-done | bytes 524304 | tf_op jit(solution)/shard_map/reduce_scatter | solution.py:171
  202.5 1.5 add_convert_fusion
  204.0 0.9 convolution_convert_fusion.1
  204.9 86.4 %all-reduce.2.cloned.1.call-done = bf16[32,1024]{1,0:T(8,128)(2,1)} async-done(((bf16[32,1024]{1,0:T(8,128)(2,1)}), bf16[32,1024]{1,0:T(8,128)(2,1)}) %all-reduce.2.cloned.1.call-update) | async-done | bytes 65552 | tf_op jit(solution)/shard_map/psum | solution.py:181
  291.4 5.2 %all_gather.11 = bf16[32,2048]{1,0:T(8,128)(2,1)S(1)} all-gather(bf16[32,1024]{1,0:T(8,128)(2,1)} %all-reduce.2.cloned.1.call-done), channel_id=1, replica_groups=mesh['seq'=16,'mp'=2] {'mp'}, dimensions={1}, use_global_device_ids=true | all-gather | bytes 196608 | tf_op jit(solution)/shard_map/all_gather | solution.py:182
  296.8 3.6 %convolution_reduce_fusion = f32[32]{0:T(128)S(1)} fusion(bf16[32,2048]{1,0:T(8,128)(2,1)S(1)} %fusion.27, bf16[2048,1000]{0,1:T(8,128)(2,1)} %param.21), kind=kOutput, calls=%fused_computation.37 | convolution fusion | flops 131103968 | bytes 4227200 | tf_op jit(solution)/shard_map/dot_general | solution.py:185
  300.4 0.7 pad_maximum_fusion.2
  301.1 41.7 %pmax.7 = f32[32]{0:T(128)} all-reduce(f32[32]{0:T(128)S(1)} %convolution_reduce_fusion), channel_id=1, replica_groups=mesh['seq'=16,'mp'=2] {'seq','mp'}, use_global_device_ids=true, to_apply=%region_17.18 | all-reduce | flops 32 | bytes 256 | tf_op jit(solution)/shard_map/pmax | solution.py:186
  (105 shorter events, 3.1 us)
Async XLA Ops:
  7.2 4.5 %copy-start = (bf16[2048,512]{1,0:T(8,128)(2,1)S(1)}, bf16[2048,512]{1,0:T(8,128)(2,1)}, u32[]{:S(2)}) copy-start(bf16[2048,512]{1,0:T(8,128)(2,1)} %param.18) | copy-start | bytes 6291460
  7.2 7.3 %copy-start.13 = (s32[32]{0:T(128)S(1)}, s32[32]{0:T(128)}, u32[]{:S(2)}) copy-start(s32[32]{0:T(128)} %param.14) | copy-start | bytes 388
  7.2 60.2 %all-gather.3.cloned.1.call-start = ((), (), s32[]{:S(2)}) async-start(), calls=%async_computation.3 | async-start | bytes 4456448 | tf_op jit(solution)/shard_map/all_gather | solution.py:86
  9.3 193.1 %reduce-scatter.2.cloned.1.call-start = ((), (), s32[]{:S(2)}) async-start(), calls=%async_computation.1 | async-start | bytes 1572864 | tf_op jit(solution)/shard_map/reduce_scatter | solution.py:171
  11.6 23.9 %copy-start.4 = (bf16[256,2048]{1,0:T(8,128)(2,1)S(1)}, bf16[256,2048]{1,0:T(8,128)(2,1)}, u32[]{:S(2)}) copy-start(bf16[256,2048]{1,0:T(8,128)(2,1)} %param.13) | copy-start | bytes 3145732
  11.6 2.9 copy-start.17
  17.2 0.6 copy-start.14
  17.9 0.6 copy-start.8
  18.0 0.6 copy-start.10
  18.7 20.9 %copy-start.9 = (f32[256,32]{0,1:T(8,128)S(1)}, f32[256,32]{0,1:T(8,128)}, u32[]{:S(2)}) copy-start(f32[256,32]{0,1:T(8,128)} %copy-done.8) | copy-start | bytes 98308
  18.7 20.9 %copy-start.11 = (f32[256,32]{0,1:T(8,128)S(1)}, f32[256,32]{0,1:T(8,128)}, u32[]{:S(2)}) copy-start(f32[256,32]{0,1:T(8,128)} %copy-done.10) | copy-start | bytes 98308
  19.5 27.7 %collective-permute-start = (bf16[256,256]{1,0:T(8,128)(2,1)}, bf16[256,256]{1,0:T(8,128)(2,1)}, u32[]{:S(2)}, u32[]{:S(2)}) collective-permute-start(bf16[256,256]{1,0:T(8,128)(2,1)} %pad_maximum_fusion.4), channel_id=1, source_target_pairs={{0,2},{2,4},{4,6},{6,8},{8,10},{10,12},{12,14},{14,16},{16,18},{18... | collective-permute-start | bytes 393224 | tf_op jit(solution)/shard_map/ppermute | solution.py:57
  22.5 26.3 %collective-permute-start.1 = (bf16[256,256]{1,0:T(8,128)(2,1)}, bf16[256,256]{1,0:T(8,128)(2,1)}, u32[]{:S(2)}, u32[]{:S(2)}) collective-permute-start(bf16[256,256]{1,0:T(8,128)(2,1)} %pad_maximum_fusion.4), channel_id=1, source_target_pairs={{0,4},{2,6},{4,8},{6,10},{8,12},{10,14},{12,16},{14,18},{16,20},{1... | collective-permute-start | bytes 393224 | tf_op jit(solution)/shard_map/ppermute | solution.py:57
  26.9 23.4 %collective-permute-start.2 = (bf16[256,256]{1,0:T(8,128)(2,1)}, bf16[256,256]{1,0:T(8,128)(2,1)}, u32[]{:S(2)}, u32[]{:S(2)}) collective-permute-start(bf16[256,256]{1,0:T(8,128)(2,1)} %pad_maximum_fusion.4), channel_id=1, source_target_pairs={{0,6},{2,8},{4,10},{6,12},{8,14},{10,16},{12,18},{14,20},{16,22},{... | collective-permute-start | bytes 393224 | tf_op jit(solution)/shard_map/ppermute | solution.py:57
  31.4 20.5 %collective-permute-start.3 = (bf16[256,256]{1,0:T(8,128)(2,1)}, bf16[256,256]{1,0:T(8,128)(2,1)}, u32[]{:S(2)}, u32[]{:S(2)}) collective-permute-start(bf16[256,256]{1,0:T(8,128)(2,1)} %pad_maximum_fusion.4), channel_id=1, source_target_pairs={{0,8},{2,10},{4,12},{6,14},{8,16},{10,18},{12,20},{14,22},{16,24},... | collective-permute-start | bytes 393224 | tf_op jit(solution)/shard_map/ppermute | solution.py:57
  35.5 7.2 %copy-start.15 = (s32[32]{0:T(128)S(1)}, s32[32]{0:T(128)}, u32[]{:S(2)}) copy-start(s32[32]{0:T(128)} %copy-done.14) | copy-start | bytes 388
  71.0 3.2 copy-start.1
  83.3 3.2 copy-start.1
  95.6 3.2 copy-start.1
  107.9 3.2 copy-start.1
  119.1 1.7 copy-start.2
  122.0 1.0 copy-start.3
  124.4 4.6 %copy-start.5 = (bf16[256,2048]{1,0:T(8,128)(2,1)S(1)}, bf16[256,2048]{1,0:T(8,128)(2,1)}, u32[]{:S(2)}) copy-start(bf16[256,2048]{1,0:T(8,128)(2,1)} %param.13) | copy-start | bytes 3145732
  129.0 75.0 %copy-start.16 = (s32[32]{0:T(128)S(1)}, s32[32]{0:T(128)}, u32[]{:S(2)}) copy-start(s32[32]{0:T(128)} %get-tuple-element.333) | copy-start | bytes 388
  129.0 75.9 %copy-start.12 = (bf16[2048]{0:T(1024)(128)(2,1)S(1)}, bf16[2048]{0:T(1024)(128)(2,1)}, u32[]{:S(2)}) copy-start(bf16[2048]{0:T(1024)(128)(2,1)} %param.20) | copy-start | bytes 12292
  129.0 162.4 %all-reduce.2.cloned.1.call-start = ((), (), s32[]{:S(2)}) async-start(), calls=%async_computation.2 | async-start | bytes 131072 | tf_op jit(solution)/shard_map/psum | solution.py:181
  204.0 138.9 %copy-start.6 = (bf16[256,1024]{1,0:T(8,128)(2,1)}, bf16[256,1024]{1,0:T(8,128)(2,1)S(1)}, u32[]{:S(2)}) copy-start(bf16[256,1024]{1,0:T(8,128)(2,1)S(1)} %add_convert_fusion) | copy-start | bytes 1572868
  296.8 46.1 %copy-start.7 = (bf16[32,2048]{1,0:T(8,128)(2,1)}, bf16[32,2048]{1,0:T(8,128)(2,1)S(1)}, u32[]{:S(2)}) copy-start(bf16[32,2048]{1,0:T(8,128)(2,1)S(1)} %fusion.27) | copy-start | bytes 393220
Sparse Core Ops, SparseCore 0:
  10.8 56.5 all-gather.2
  129.1 73.2 reduce-scatter.1
  206.9 84.4 all-reduce.1
where the time goes:
time: 350 us; the launch traced here: 349 us
  waiting for transfers between devices  172 us (49%)
  matrix products  48.3 us (14%)
  blocking collectives  46.9 us (13%)
  local copies, waits for them, and re-layouts  26.9 us (8%)
  between operations  19.7 us (6%)
  other arithmetic  19.6 us (6%)
  starting transfers between devices  15.5 us (4%)
    psum x1, waiting for transfers between devices, per_device(): last_part = lax.psum(last_part, 'seq')  86.4 us
    reduce_scatter x1, waiting for transfers between devices, per_device(): lax.psum_scatter(mixture.astype(jnp.bfloat16), 'mp', scatter_dimension=1,...  71.8 us
    pmax x1, blocking collectives, per_device(): greatest = lax.pmax(jnp.max(logits, -1), ('seq', 'mp'))  41.7 us
    dot_general x5, matrix products, attend(): jnp.einsum('grqn,ngd->grqd', weights.astype(jnp.bfloat16), val_rows, pref...  27.2 us
    ppermute x4, starting transfers between devices, shifted_back(): return lax.ppermute(block, axis, route)  15.3 us
    all_gather x1, waiting for transfers between devices, per_device(): all_prefix = lax.all_gather(own_prefix, 'seq', axis=0)  13.9 us
    while x25, local copies, waits for them, and re-layouts  8.14 us
    reduce_sum x5, other arithmetic, attend(): new_sum = old_sum * factor + jnp.sum(weights, -1)  7.48 us
  transfers between devices with their start and end apart: 7, of which 3 were waited for; matrix products, arithmetic and copies ran while one was open for 7% of the time, Pallas kernels for 0%

commit v1 on v0

--- a/solution.py
+++ b/solution.py
@@ -178,7 +178,7 @@
         jnp.bfloat16
     )
     last_part = jnp.dot(onehot, hidden, preferred_element_type=jnp.float32).astype(jnp.bfloat16)
-    last_part = lax.psum(last_part, "seq")
+    last_part = jnp.sum(lax.all_gather(last_part, "seq"), axis=0)
     last_rows = lax.all_gather(last_part, "mp", axis=1, tiled=True).astype(jnp.float32)
     inv_rms = lax.rsqrt(jnp.mean(last_rows * last_rows, -1, keepdims=True) + epsilon)
     last_normed = (last_rows * final_gain.astype(jnp.float32) * inv_rms).astype(jnp.bfloat16)

time: 350 us -> 301 us (0.86)
  waiting for transfers between devices: 172 us -> 124 us
    psum x1 -> x0, waiting for transfers between devices: 86.4 us -> none  [per_device(): last_part = lax.psum(last_part, 'seq')]
    all_gather x0 -> x1, waiting for transfers between devices: none -> 38.5 us  [per_device(): last_part = jnp.sum(lax.all_gather(last_part, 'seq'), axis=0)]
  transfers between devices with their start and end apart: 7 -> 7, of which waited for: 3 -> 3; matrix products, arithmetic and copies ran while one was open for 7% -> 8% of each run, Pallas kernels for 0% -> 0%
where the time goes in v1:
time: 301 us; the launch traced here: 300 us
  waiting for transfers between devices  124 us (41%)
  matrix products  48.3 us (16%)
  blocking collectives  43.7 us (15%)
  local copies, waits for them, and re-layouts  26.9 us (9%)
  other arithmetic  21 us (7%)
  between operations  19.7 us (7%)
  starting transfers between devices  15.5 us (5%)
    reduce_scatter x1, waiting for transfers between devices, per_device(): lax.psum_scatter(mixture.astype(jnp.bfloat16), 'mp', scatter_dimension=1,...  71.8 us
    pmax x1, blocking collectives, per_device(): greatest = lax.pmax(jnp.max(logits, -1), ('seq', 'mp'))  38.8 us
    all_gather x1, waiting for transfers between devices, per_device(): last_part = jnp.sum(lax.all_gather(last_part, 'seq'), axis=0)  38.5 us
    dot_general x5, matrix products, attend(): jnp.einsum('grqn,ngd->grqd', weights.astype(jnp.bfloat16), val_rows, pref...  27.2 us
    ppermute x4, starting transfers between devices, shifted_back(): return lax.ppermute(block, axis, route)  15.3 us
    all_gather x1, waiting for transfers between devices, per_device(): all_prefix = lax.all_gather(own_prefix, 'seq', axis=0)  13.9 us
    while x25, local copies, waits for them, and re-layouts  8.14 us
    reduce_sum x5, other arithmetic, attend(): new_sum = old_sum * factor + jnp.sum(weights, -1)  7.48 us
  transfers between devices with their start and end apart: 7, of which 3 were waited for; matrix products, arithmetic and copies ran while one was open for 8% of the time, Pallas kernels for 0%

profile of v1, /device:TPU:0, one launch (start us, length us, event | category | flops | bytes accessed | tf_op | source)
XLA Modules:
  0.0 299.7 jit_solution(13687479178398181889)
XLA Ops:
  7.3 1.3 constant_dynamic-slice_fusion.5
  8.6 0.7 pad_maximum_fusion.1
  9.4 0.7 convert_element_type.77
  10.1 1.5 multiply_reduce_fusion
  11.6 2.0 fusion.24
  13.7 0.7 slice.63
  14.7 1.1 copy.41
  15.9 1.2 add_subtract_fusion
  18.0 0.5 copy-done.8
  18.8 0.7 pad_maximum_fusion.4
  19.5 3.0 %collective-permute-start = (bf16[256,256]{1,0:T(8,128)(2,1)}, bf16[256,256]{1,0:T(8,128)(2,1)}, u32[]{:S(2)}, u32[]{:S(2)}) collective-permute-start(bf16[256,256]{1,0:T(8,128)(2,1)} %pad_maximum_fusion.4), channel_id=1, source_target_pairs={{0,2},{2,4},{4,6},{6,8},{8,10},{10,12},{12,14},{14,16},{16,18},{18... | collective-permute-start | bytes 393224 | tf_op jit(solution)/shard_map/ppermute | solution.py:57
  22.5 4.4 %collective-permute-start.1 = (bf16[256,256]{1,0:T(8,128)(2,1)}, bf16[256,256]{1,0:T(8,128)(2,1)}, u32[]{:S(2)}, u32[]{:S(2)}) collective-permute-start(bf16[256,256]{1,0:T(8,128)(2,1)} %pad_maximum_fusion.4), channel_id=1, source_target_pairs={{0,4},{2,6},{4,8},{6,10},{8,12},{10,14},{12,16},{14,18},{16,20},{1... | collective-permute-start | bytes 393224 | tf_op jit(solution)/shard_map/ppermute | solution.py:57
  26.9 4.4 %collective-permute-start.2 = (bf16[256,256]{1,0:T(8,128)(2,1)}, bf16[256,256]{1,0:T(8,128)(2,1)}, u32[]{:S(2)}, u32[]{:S(2)}) collective-permute-start(bf16[256,256]{1,0:T(8,128)(2,1)} %pad_maximum_fusion.4), channel_id=1, source_target_pairs={{0,6},{2,8},{4,10},{6,12},{8,14},{10,16},{12,18},{14,20},{16,22},{... | collective-permute-start | bytes 393224 | tf_op jit(solution)/shard_map/ppermute | solution.py:57
  31.4 3.5 %collective-permute-start.3 = (bf16[256,256]{1,0:T(8,128)(2,1)}, bf16[256,256]{1,0:T(8,128)(2,1)}, u32[]{:S(2)}, u32[]{:S(2)}) collective-permute-start(bf16[256,256]{1,0:T(8,128)(2,1)} %pad_maximum_fusion.4), channel_id=1, source_target_pairs={{0,8},{2,10},{4,12},{6,14},{8,16},{10,18},{12,20},{14,22},{16,24},... | collective-permute-start | bytes 393224 | tf_op jit(solution)/shard_map/ppermute | solution.py:57
  34.8 0.7 bitcast_dynamic-update-slice_fusion.4
  35.5 4.0 %fusion.25 = f32[256,1024]{0,1:T(8,128)S(1)} fusion(bf16[2048,1024]{1,0:T(8,128)(2,1)} %param.17, f32[2048]{0:T(1024)S(1)} %convert_element_type.77, f32[256]{0:T(256)} %copy-done.17, bf16[256,2048]{1,0:T(8,128)(2,1)S(1)} %copy-done.4), kind=kOutput, calls=%fused_computation.46 | convolution fusion | flops 1075838976 | bytes 6300672 | tf_op jit(solution)/shard_map/dot_general | solution.py:115
  39.7 0.6 fusion.32
  40.3 0.6 slice.50
  42.8 0.6 dynamic_slice.31
  47.2 1.6 bitcast_dynamic-update-slice_fusion.3
  48.8 1.6 bitcast_dynamic-update-slice_fusion.2
  50.3 1.6 bitcast_dynamic-update-slice_fusion.1
  51.9 1.6 bitcast_dynamic-update-slice_fusion
  53.5 13.9 %all-gather.5.cloned.1.call-done = bf16[64,128,256]{2,1,0:T(8,128)(2,1)} async-done(((bf16[4,128,256]{2,1,0:T(8,128)(2,1)}), bf16[64,128,256]{2,1,0:T(8,128)(2,1)}) %all-gather.5.cloned.1.call-update) | async-done | bytes 4194320 | tf_op jit(solution)/shard_map/all_gather | solution.py:86
  67.4 1.1 broadcast_in_dim.52
  68.6 49.2 %while.31 = (s32[]{:T(128)}, f32[2,8,256]{2,1,0:T(8,128)S(1)}, f32[2,8,256]{2,1,0:T(8,128)S(1)}, f32[2,8,256,64]{2,3,1,0:T(8,128)}, s32[]{:T(128)}, /*index=5*/s...) while((s32[]{:T(128)}, f32[2,8,256]{2,1,0:T(8,128)S(1)}, ...), condition=%wide.region_7.8_spmd, body=%wide.region_4.7_spmd.sunk | while | flops 560472320 | bytes 63441352 | solution.py:144
  68.6 1.0 constant_dynamic-slice_fusion.8
  69.7 1.3 bitcast_reduce_fusion.2
  71.0 1.7 fusion.66
  72.7 1.5 copy-done.1
  74.4 6.5 %fusion.67 = f32[2,8,256,64]{2,3,1,0:T(8,128)} fusion(bf16[512,2,64,1]{0,2,3,1:T(8,128)(2,1)S(1)} %bitcast.124, f32[2,512,256,8]{2,1,3,0:T(8,128)} %copy-done.1, f32[2,8,256]{2,1,0:T(8,128)S(1)} %max.14, pred[256]{0:T(512)(128)(4,1)S(1)} %broadcast_compare_fusion.2, f32[2,8,256,64]{2,3,1,0:T(8,128)} %get-tuple-element.501, ...), kind=kOutput, calls=%fused_computation.9.clone.1 | convolution fusion | flops 277348352 | bytes 10649856 | tf_op jit(solution)/shard_map/while/body/grqn,ngd->grqd/dot_general | solution.py:48
  80.9 1.0 constant_dynamic-slice_fusion.8
  82.0 1.3 bitcast_reduce_fusion.2
  83.3 1.7 fusion.66
  85.0 1.5 copy-done.1
  86.7 6.5 %fusion.67 = f32[2,8,256,64]{2,3,1,0:T(8,128)} fusion(bf16[512,2,64,1]{0,2,3,1:T(8,128)(2,1)S(1)} %bitcast.124, f32[2,512,256,8]{2,1,3,0:T(8,128)} %copy-done.1, f32[2,8,256]{2,1,0:T(8,128)S(1)} %max.14, pred[256]{0:T(512)(128)(4,1)S(1)} %broadcast_compare_fusion.2, f32[2,8,256,64]{2,3,1,0:T(8,128)} %get-tuple-element.501, ...), kind=kOutput, calls=%fused_computation.9.clone.1 | convolution fusion | flops 277348352 | bytes 10649856 | tf_op jit(solution)/shard_map/while/body/grqn,ngd->grqd/dot_general | solution.py:48
  93.2 1.0 constant_dynamic-slice_fusion.8
  94.3 1.3 bitcast_reduce_fusion.2
  95.6 1.7 fusion.66
  97.3 1.5 copy-done.1
  99.0 6.5 %fusion.67 = f32[2,8,256,64]{2,3,1,0:T(8,128)} fusion(bf16[512,2,64,1]{0,2,3,1:T(8,128)(2,1)S(1)} %bitcast.124, f32[2,512,256,8]{2,1,3,0:T(8,128)} %copy-done.1, f32[2,8,256]{2,1,0:T(8,128)S(1)} %max.14, pred[256]{0:T(512)(128)(4,1)S(1)} %broadcast_compare_fusion.2, f32[2,8,256,64]{2,3,1,0:T(8,128)} %get-tuple-element.501, ...), kind=kOutput, calls=%fused_computation.9.clone.1 | convolution fusion | flops 277348352 | bytes 10649856 | tf_op jit(solution)/shard_map/while/body/grqn,ngd->grqd/dot_general | solution.py:48
  105.5 1.0 constant_dynamic-slice_fusion.8
  106.6 1.3 bitcast_reduce_fusion.2
  108.0 1.7 fusion.66
  109.6 1.5 copy-done.1
  111.3 6.5 %fusion.67 = f32[2,8,256,64]{2,3,1,0:T(8,128)} fusion(bf16[512,2,64,1]{0,2,3,1:T(8,128)(2,1)S(1)} %bitcast.124, f32[2,512,256,8]{2,1,3,0:T(8,128)} %copy-done.1, f32[2,8,256]{2,1,0:T(8,128)S(1)} %max.14, pred[256]{0:T(512)(128)(4,1)S(1)} %broadcast_compare_fusion.2, f32[2,8,256,64]{2,3,1,0:T(8,128)} %get-tuple-element.501, ...), kind=kOutput, calls=%fused_computation.9.clone.1 | convolution fusion | flops 277348352 | bytes 10649856 | tf_op jit(solution)/shard_map/while/body/grqn,ngd->grqd/dot_general | solution.py:48
  117.8 5.3 %while.32 = (s32[]{:T(128)}, f32[2,8,256]{2,1,0:T(8,128)S(1)}, f32[2,8,256]{2,1,0:T(8,128)S(1)}, f32[2,8,256,64]{2,3,1,0:T(8,128)}, s32[]{:T(128)}, /*index=5*/s...) while((s32[]{:T(128)}, f32[2,8,256]{2,1,0:T(8,128)S(1)}, ...), condition=%wide.region_12.13_spmd.clone, body=%wide.region_8.12_spmd.clone.sunk | while | flops 280789248 | bytes 25043356 | solution.py:162
  118.1 0.9 constant_dynamic-slice_fusion.9
  119.1 0.8 fusion.73
  119.9 0.9 fusion.74
  120.8 1.2 fusion.75
  122.0 1.0 copy-done.3
  123.1 1.3 divide_convert_fusion
  124.4 4.6 %convolution_convert_fusion = bf16[256,2048]{1,0:T(8,128)(2,1)} fusion(bf16[256,1024]{0,1:T(8,128)(2,1)S(1)} %bitcast.128, bf16[1024,2048]{1,0:T(8,128)(2,1)} %param.19), kind=kOutput, calls=%fused_computation.33 | convolution fusion | flops 1074266112 | bytes 5767168 | tf_op jit(solution)/shard_map/dot_general | solution.py:170
  129.1 1.6 convert_element_type.75
  130.6 71.8 %reduce-scatter.2.cloned.1.call-done = bf16[256,1024]{1,0:T(8,128)(2,1)} async-done(((bf16[256,2048]{1,0:T(8,128)(2,1)}), bf16[256,1024]{1,0:T(8,128)(2,1)}) %reduce-scatter.2.cloned.1.call-update) | async-done | bytes 524304 | tf_op jit(solution)/shard_map/reduce_scatter | solution.py:171
  202.5 1.5 add_convert_fusion
  204.0 0.9 convolution_convert_fusion.1
  204.9 38.5 %all-gather.7.cloned.1.call-done = bf16[512,1024]{1,0:T(8,128)(2,1)} async-done(((bf16[32,1024]{1,0:T(8,128)(2,1)}), bf16[512,1024]{1,0:T(8,128)(2,1)}) %all-gather.7.cloned.1.call-update) | async-done | bytes 1048592 | tf_op jit(solution)/shard_map/all_gather | solution.py:181
  243.4 1.4 reduce_sum.81
  244.8 4.9 %all_gather.19 = bf16[32,2048]{1,0:T(8,128)(2,1)S(1)} all-gather(bf16[32,1024]{1,0:T(8,128)(2,1)S(1)} %reduce_sum.81), channel_id=1, replica_groups=mesh['seq'=16,'mp'=2] {'mp'}, dimensions={1}, use_global_device_ids=true | all-gather | bytes 196608 | tf_op jit(solution)/shard_map/all_gather | solution.py:182
  250.0 3.6 %convolution_reduce_fusion = f32[32]{0:T(128)S(1)} fusion(bf16[32,2048]{1,0:T(8,128)(2,1)S(1)} %fusion.27, bf16[2048,1000]{0,1:T(8,128)(2,1)} %param.21), kind=kOutput, calls=%fused_computation.37 | convolution fusion | flops 131103968 | bytes 4227200 | tf_op jit(solution)/shard_map/dot_general | solution.py:185
  253.6 0.7 pad_maximum_fusion.2
  254.3 38.8 %pmax.7 = f32[32]{0:T(128)} all-reduce(f32[32]{0:T(128)S(1)} %convolution_reduce_fusion), channel_id=1, replica_groups=mesh['seq'=16,'mp'=2] {'seq','mp'}, use_global_device_ids=true, to_apply=%region_17.18 | all-reduce | flops 32 | bytes 256 | tf_op jit(solution)/shard_map/pmax | solution.py:186
  (106 shorter events, 3.6 us)
Async XLA Ops:
  7.2 4.5 %copy-start = (bf16[2048,512]{1,0:T(8,128)(2,1)S(1)}, bf16[2048,512]{1,0:T(8,128)(2,1)}, u32[]{:S(2)}) copy-start(bf16[2048,512]{1,0:T(8,128)(2,1)} %param.18) | copy-start | bytes 6291460
  7.2 7.3 %copy-start.13 = (s32[32]{0:T(128)S(1)}, s32[32]{0:T(128)}, u32[]{:S(2)}) copy-start(s32[32]{0:T(128)} %param.14) | copy-start | bytes 388
  7.2 60.2 %all-gather.5.cloned.1.call-start = ((), (), s32[]{:S(2)}) async-start(), calls=%async_computation.2 | async-start | bytes 4456448 | tf_op jit(solution)/shard_map/all_gather | solution.py:86
  9.3 193.1 %reduce-scatter.2.cloned.1.call-start = ((), (), s32[]{:S(2)}) async-start(), calls=%async_computation.1 | async-start | bytes 1572864 | tf_op jit(solution)/shard_map/reduce_scatter | solution.py:171
  11.6 23.9 %copy-start.4 = (bf16[256,2048]{1,0:T(8,128)(2,1)S(1)}, bf16[256,2048]{1,0:T(8,128)(2,1)}, u32[]{:S(2)}) copy-start(bf16[256,2048]{1,0:T(8,128)(2,1)} %param.13) | copy-start | bytes 3145732
  11.6 2.9 copy-start.17
  17.2 0.6 copy-start.14
  17.9 0.6 copy-start.8
  18.0 0.6 copy-start.10
  18.7 20.9 %copy-start.9 = (f32[256,32]{0,1:T(8,128)S(1)}, f32[256,32]{0,1:T(8,128)}, u32[]{:S(2)}) copy-start(f32[256,32]{0,1:T(8,128)} %copy-done.8) | copy-start | bytes 98308
  18.7 20.9 %copy-start.11 = (f32[256,32]{0,1:T(8,128)S(1)}, f32[256,32]{0,1:T(8,128)}, u32[]{:S(2)}) copy-start(f32[256,32]{0,1:T(8,128)} %copy-done.10) | copy-start | bytes 98308
  19.5 27.7 %collective-permute-start = (bf16[256,256]{1,0:T(8,128)(2,1)}, bf16[256,256]{1,0:T(8,128)(2,1)}, u32[]{:S(2)}, u32[]{:S(2)}) collective-permute-start(bf16[256,256]{1,0:T(8,128)(2,1)} %pad_maximum_fusion.4), channel_id=1, source_target_pairs={{0,2},{2,4},{4,6},{6,8},{8,10},{10,12},{12,14},{14,16},{16,18},{18... | collective-permute-start | bytes 393224 | tf_op jit(solution)/shard_map/ppermute | solution.py:57
  22.5 26.3 %collective-permute-start.1 = (bf16[256,256]{1,0:T(8,128)(2,1)}, bf16[256,256]{1,0:T(8,128)(2,1)}, u32[]{:S(2)}, u32[]{:S(2)}) collective-permute-start(bf16[256,256]{1,0:T(8,128)(2,1)} %pad_maximum_fusion.4), channel_id=1, source_target_pairs={{0,4},{2,6},{4,8},{6,10},{8,12},{10,14},{12,16},{14,18},{16,20},{1... | collective-permute-start | bytes 393224 | tf_op jit(solution)/shard_map/ppermute | solution.py:57
  26.9 23.4 %collective-permute-start.2 = (bf16[256,256]{1,0:T(8,128)(2,1)}, bf16[256,256]{1,0:T(8,128)(2,1)}, u32[]{:S(2)}, u32[]{:S(2)}) collective-permute-start(bf16[256,256]{1,0:T(8,128)(2,1)} %pad_maximum_fusion.4), channel_id=1, source_target_pairs={{0,6},{2,8},{4,10},{6,12},{8,14},{10,16},{12,18},{14,20},{16,22},{... | collective-permute-start | bytes 393224 | tf_op jit(solution)/shard_map/ppermute | solution.py:57
  31.4 20.5 %collective-permute-start.3 = (bf16[256,256]{1,0:T(8,128)(2,1)}, bf16[256,256]{1,0:T(8,128)(2,1)}, u32[]{:S(2)}, u32[]{:S(2)}) collective-permute-start(bf16[256,256]{1,0:T(8,128)(2,1)} %pad_maximum_fusion.4), channel_id=1, source_target_pairs={{0,8},{2,10},{4,12},{6,14},{8,16},{10,18},{12,20},{14,22},{16,24},... | collective-permute-start | bytes 393224 | tf_op jit(solution)/shard_map/ppermute | solution.py:57
  35.5 7.2 %copy-start.15 = (s32[32]{0:T(128)S(1)}, s32[32]{0:T(128)}, u32[]{:S(2)}) copy-start(s32[32]{0:T(128)} %copy-done.14) | copy-start | bytes 388
  71.0 3.2 %copy-start.1 = (f32[2,512,256,8]{2,1,3,0:T(8,128)}, f32[2,512,256,8]{2,1,3,0:T(8,128)S(1)}, u32[]{:S(2)}) copy-start(f32[2,512,256,8]{2,1,3,0:T(8,128)S(1)} %get-tuple-element.460) | copy-start | bytes 25165828 | tf_op jit(solution)/shard_map/while
  83.3 3.2 %copy-start.1 = (f32[2,512,256,8]{2,1,3,0:T(8,128)}, f32[2,512,256,8]{2,1,3,0:T(8,128)S(1)}, u32[]{:S(2)}) copy-start(f32[2,512,256,8]{2,1,3,0:T(8,128)S(1)} %get-tuple-element.460) | copy-start | bytes 25165828 | tf_op jit(solution)/shard_map/while
  95.6 3.2 %copy-start.1 = (f32[2,512,256,8]{2,1,3,0:T(8,128)}, f32[2,512,256,8]{2,1,3,0:T(8,128)S(1)}, u32[]{:S(2)}) copy-start(f32[2,512,256,8]{2,1,3,0:T(8,128)S(1)} %get-tuple-element.460) | copy-start | bytes 25165828 | tf_op jit(solution)/shard_map/while
  107.9 3.2 %copy-start.1 = (f32[2,512,256,8]{2,1,3,0:T(8,128)}, f32[2,512,256,8]{2,1,3,0:T(8,128)S(1)}, u32[]{:S(2)}) copy-start(f32[2,512,256,8]{2,1,3,0:T(8,128)S(1)} %get-tuple-element.460) | copy-start | bytes 25165828 | tf_op jit(solution)/shard_map/while
  119.1 1.7 copy-start.2
  122.0 1.0 copy-start.3
  124.4 4.6 %copy-start.5 = (bf16[256,2048]{1,0:T(8,128)(2,1)S(1)}, bf16[256,2048]{1,0:T(8,128)(2,1)}, u32[]{:S(2)}) copy-start(bf16[256,2048]{1,0:T(8,128)(2,1)} %param.13) | copy-start | bytes 3145732
  129.0 75.0 %copy-start.16 = (s32[32]{0:T(128)S(1)}, s32[32]{0:T(128)}, u32[]{:S(2)}) copy-start(s32[32]{0:T(128)} %get-tuple-element.333) | copy-start | bytes 388
  129.0 75.9 %copy-start.12 = (bf16[2048]{0:T(1024)(128)(2,1)S(1)}, bf16[2048]{0:T(1024)(128)(2,1)}, u32[]{:S(2)}) copy-start(bf16[2048]{0:T(1024)(128)(2,1)} %param.20) | copy-start | bytes 12292
  129.0 114.4 %all-gather.7.cloned.1.call-start = ((), (), s32[]{:S(2)}) async-start(), calls=%async_computation.3 | async-start | bytes 1114112 | tf_op jit(solution)/shard_map/all_gather | solution.py:181
  204.0 89.2 %copy-start.6 = (bf16[256,1024]{1,0:T(8,128)(2,1)}, bf16[256,1024]{1,0:T(8,128)(2,1)S(1)}, u32[]{:S(2)}) copy-start(bf16[256,1024]{1,0:T(8,128)(2,1)S(1)} %add_convert_fusion) | copy-start | bytes 1572868
  250.0 43.2 %copy-start.7 = (bf16[32,2048]{1,0:T(8,128)(2,1)}, bf16[32,2048]{1,0:T(8,128)(2,1)S(1)}, u32[]{:S(2)}) copy-start(bf16[32,2048]{1,0:T(8,128)(2,1)S(1)} %fusion.27) | copy-start | bytes 393220
Sparse Core Ops, SparseCore 0:
  10.8 56.5 all-gather.4
  129.1 73.2 reduce-scatter.1
  205.4 37.9 all-gather.6
